TPU v7x, 128 devices: a whole 4x4x4 slice. The times are simulated.
128 devices in a mesh: seq: 16 (over x_hi, z, core), kvh: 8 (over x_lo, y).
Axes of the slice: x: 4 (x_hi: 2, x_lo: 2; x = x_hi * 2 + x_lo), y: 4, z: 4, core: 2. Of those that a mesh axis runs over, the one named last changes fastest.
Arguments:
- normed: bfloat16 [4096, 4096], P('seq'), may hold values from -8 to 8
- w_query: bfloat16 [4096, 4096], P(None, 'kvh'), may hold values from -1 to 1, as said below
- w_key: bfloat16 [4096, 1024], P(None, 'kvh'), may hold values from -1 to 1, as said below
- w_value: bfloat16 [4096, 1024], P(None, 'kvh'), may hold values from -0.09375 to 0.09375
- positions: int32 [4096], P('seq'), may hold values from 0 to 4222, as said below
- block_mask: int32 [32, 32], P('seq'), may hold values from 0 to 1, as said below
- grad_attn: bfloat16 [4096, 4096], P('seq', 'kvh'), may hold values from -6 to 6
Outputs:
- grad_normed: bfloat16 [4096, 4096], P('seq', 'kvh')
- grad_wq: float32 [4096, 4096], P('seq', 'kvh')
- grad_wk: float32 [4096, 1024], P('seq', 'kvh')
- grad_wv: float32 [4096, 1024], P('seq', 'kvh')
Inputs may be any that keep to these rules, and one draw needn't show every extreme that they name: Within a block positions rise by one per token; block b starts between b * 128 and (b + 1) * 128 - 1, block 0 at 0, the last block at its latest start. `block_mask`: the diagonal is 1; a block may read only blocks of earlier rounds besides itself; entries for earlier rounds are 0 or 1. `w_query`: entries of about 4096^(-1/2) in size. `w_key`: entries of about 4096^(-1/2) in size.
All inputs are finite; a program needn't handle non-finite values.
Results may differ from a plain program's by a relative error of at most 0.019.
The roundings to bfloat16 on the way count: a program that leaves them out, or rounds other values in their place, can miss the bound.
Values may be sent and summed in bfloat16 or wider, within the bound.
No kernel may reach another device: no remote copies, remote signals or barrier semaphores. Data moves between devices by JAX's collectives and lax.ppermute only.
A program may use at most 128 MiB of HBM per device.

v0:
```python
import jax
import jax.numpy as jnp
from jax import lax
from jax.sharding import PartitionSpec as P

HEAD = 128
BLOCK = 128


THETA = 500000.0


def rotate(values, positions, rotation_sign):
    tok_rows = values.shape[0]
    head_count = values.shape[1] // HEAD
    half_size = HEAD // 2
    pieces = values.reshape(tok_rows, head_count, HEAD)
    frequency = THETA ** (-(jnp.arange(half_size, dtype=jnp.float32) * (2.0 / HEAD)))
    angles = positions.astype(jnp.float32)[:, None] * frequency[None, :]
    cosine = jnp.cos(angles)[:, None, :]
    sine_part = rotation_sign * jnp.sin(angles)[:, None, :]
    lower_half = pieces[:, :, :half_size]
    upper_half = pieces[:, :, half_size:]
    turned = jnp.concatenate(
        [
            lower_half * cosine - upper_half * sine_part,
            upper_half * cosine + lower_half * sine_part,
        ],
        axis=2,
    )
    return turned.reshape(tok_rows, head_count * HEAD)


def visible(mask_table, query_block0, query_count, key_count):
    query_local = jnp.arange(query_count)
    key_local = jnp.arange(key_count)
    query_block = query_block0 + query_local // BLOCK
    key_block = key_local // BLOCK
    allowed = jnp.repeat(jnp.repeat(mask_table, BLOCK, axis=0), BLOCK, axis=1) == 1
    inner_ok = (key_local % BLOCK)[None, :] <= (query_local % BLOCK)[:, None]
    return allowed & ((query_block[:, None] != key_block[None, :]) | inner_ok)


def product(form, left, right):
    return jnp.einsum(form, left, right, preferred_element_type=jnp.float32)


def masked_scores(queries, keys, seen):
    scores = product("tgd,sd->gts", queries, keys) * HEAD ** (-0.5)
    return jnp.where(seen[None], scores, -1e30)


def softmax_stats(queries, keys, values, grad_heads, seen):
    scores = masked_scores(queries, keys, seen)
    row_max = jnp.max(scores, axis=2, keepdims=True)
    log_total = row_max[:, :, 0] + jnp.log(jnp.sum(jnp.exp(scores - row_max), axis=2))
    weights = jnp.where(seen[None], jnp.exp(scores - log_total[:, :, None]), 0.0).astype(
        jnp.bfloat16
    )
    outputs = product("gts,sd->gtd", weights, values)
    row_dots = jnp.sum(outputs * jnp.transpose(grad_heads.astype(jnp.float32), (1, 0, 2)), axis=2)
    return (log_total, row_dots)


def attention_grads(queries, keys, values, grad_heads, seen, log_total, row_dots):
    scores = masked_scores(queries, keys, seen)
    probs = jnp.where(seen[None], jnp.exp(scores - log_total[:, :, None]), 0.0)
    weights = probs.astype(jnp.bfloat16)
    grad_probs = product("tgd,sd->gts", grad_heads, values)
    grad_scores = (probs * (grad_probs - row_dots[:, :, None]) * HEAD ** (-0.5)).astype(
        jnp.bfloat16
    )
    grad_query = product("gts,sd->tgd", grad_scores, keys)
    grad_key = product("gts,tgd->sd", grad_scores, queries)
    grad_value = product("gts,tgd->sd", weights, grad_heads)
    return (grad_query, grad_key, grad_value)


def body(normed, w_query, w_key, w_value, positions, block_mask, grad_attn):
    tok_rows = normed.shape[0]
    group_size = w_query.shape[1] // w_key.shape[1]
    width_query = group_size * HEAD
    blk_local = tok_rows // BLOCK
    my_index = lax.axis_index("seq")
    queries = rotate(
        jnp.dot(normed, w_query, preferred_element_type=jnp.float32), positions, 1.0
    ).astype(jnp.bfloat16)
    keys = rotate(
        jnp.dot(normed, w_key, preferred_element_type=jnp.float32), positions, 1.0
    ).astype(jnp.bfloat16)
    values = jnp.dot(normed, w_value, preferred_element_type=jnp.float32).astype(jnp.bfloat16)
    keys_all, values_all = (
        lax.all_gather(keys, "seq", axis=0, tiled=True),
        lax.all_gather(values, "seq", axis=0, tiled=True),
    )
    seen = visible(block_mask, my_index * blk_local, tok_rows, keys_all.shape[0])
    total_parts = []
    dots_parts = []
    query_heads = queries.reshape(tok_rows, group_size, HEAD)
    grad_heads = grad_attn.reshape(tok_rows, group_size, HEAD)
    log_total, row_dots = softmax_stats(query_heads, keys_all, values_all, grad_heads, seen)
    grad_query, grad_key, grad_value = attention_grads(
        query_heads, keys_all, values_all, grad_heads, seen, log_total, row_dots
    )
    query_parts = grad_query.reshape(tok_rows, width_query)
    total_parts.append(log_total.T)
    dots_parts.append(row_dots.T)
    key_total, value_total = (
        lax.psum_scatter(
            grad_key.astype(jnp.bfloat16), "seq", scatter_dimension=0, tiled=True
        ).astype(jnp.float32),
        lax.psum_scatter(
            grad_value.astype(jnp.bfloat16), "seq", scatter_dimension=0, tiled=True
        ).astype(jnp.float32),
    )
    query_grad = rotate(query_parts, positions, -1.0).astype(jnp.bfloat16)
    key_grad = rotate(key_total, positions, -1.0).astype(jnp.bfloat16)
    value_grad = value_total.astype(jnp.bfloat16)
    joined = jnp.concatenate([query_grad, key_grad, value_grad], axis=1)
    weight_grads = lax.psum_scatter(
        lax.dot_general(
            normed, joined, (((0,), (0,)), ((), ())), preferred_element_type=jnp.float32
        ).astype(jnp.bfloat16),
        "seq",
        scatter_dimension=0,
        tiled=True,
    ).astype(jnp.float32)
    query_cols = query_grad.shape[1]
    key_cols = key_grad.shape[1]
    grad_wq = weight_grads[:, :query_cols]
    grad_wk = weight_grads[:, query_cols : query_cols + key_cols]
    grad_wv = weight_grads[:, query_cols + key_cols :]
    contract = (((1,), (1,)), ((), ()))
    partial_input = lax.dot_general(
        query_grad, w_query, contract, preferred_element_type=jnp.float32
    )
    partial_input = partial_input + lax.dot_general(
        key_grad, w_key, contract, preferred_element_type=jnp.float32
    )
    partial_input = partial_input + lax.dot_general(
        value_grad, w_value, contract, preferred_element_type=jnp.float32
    )
    grad_normed = lax.psum_scatter(
        partial_input.astype(jnp.bfloat16), "kvh", scatter_dimension=1, tiled=True
    )
    return (grad_normed, grad_wq, grad_wk, grad_wv)


def solution(mesh):
    in_specs = (
        P("seq", None),
        P(None, "kvh"),
        P(None, "kvh"),
        P(None, "kvh"),
        P("seq"),
        P("seq", None),
        P("seq", "kvh"),
    )
    out_specs = (P("seq", "kvh"), P("seq", "kvh"), P("seq", "kvh"), P("seq", "kvh"))
    return jax.shard_map(body, mesh=mesh, in_specs=in_specs, out_specs=out_specs, check_vma=False)
```

profile of v0, /device:TPU:0, one launch (start us, length us, event | category | flops | bytes accessed | tf_op | source)
XLA Modules:
  0.0 413.1 jit_solution(13094747481903445248)
XLA Ops:
  7.2 0.8 convert_element_type.52
  8.1 0.7 copy-done
  8.8 2.1 convolution_bitcast_fusion.3
  10.9 0.3 fusion.34
  11.2 0.6 pad_maximum_fusion.2
  11.9 2.5 convolution_convert_fusion.1
  14.5 1.2 broadcast_multiply_fusion
  15.8 0.6 fusion.37
  16.4 3.4 fusion.55
  19.8 0.2 reshape.293
  20.0 1.1 fusion.53
  21.1 0.6 and_select_fusion
  21.7 0.7 broadcast_compare_fusion
  22.6 0.6 copy.63
  23.2 0.8 copy.31
  24.1 1.9 subtract_convert_fusion.1
  26.0 2.5 bitcast_and_fusion
  28.5 28.9 %all-gather.6.cloned.1.call-done = bf16[4096,1,128]{0,2,1:T(8,128)(2,1)} async-done(((bf16[256,1,128]{0,2,1:T(8,128)(2,1)}), bf16[4096,1,128]{0,2,1:T(8,128)(2,1)}) %all-gather.6.cloned.1.call-update) | async-done | bytes 1048592 | tf_op jit(solution)/shard_map/all_gather | solution.py:93
  57.4 4.5 %fusion.4 = (f32[4,256]{1,0:T(4,128)S(1)}, f32[4096,256,4]{1,0,2:T(8,128)S(1)}) fusion(pred[256,4096]{0,1:T(8,128)(4,1)S(1)} %bitcast_and_fusion, bf16[256,4,64]{2,0,1:T(8,128)(2,1)} %get-tuple-element.13, bf16[256,4,64]{2,0,1:T(8,128)(2,1)S(1)} %get-tuple-element.12, bf16[4096,1,128]{0,2,1:T(8,128)(2,1)} %all-gather.6.cloned.1.call-done), kind=kOutput, calls=%fused_computation.8 | convolution fusion | flops 1086848000 | bytes 19140608 | tf_op jit(solution)/shard_map/tgd,sd->gts/dot_general | solution.py:45
  61.9 3.7 exponential_reduce_fusion
  65.5 2.1 copy-done.2
  67.6 37.1 %all-gather.4.cloned.1.call-done = bf16[4096,128]{1,0:T(8,128)(2,1)} async-done(((bf16[256,128]{1,0:T(8,128)(2,1)}), bf16[4096,128]{1,0:T(8,128)(2,1)}) %all-gather.4.cloned.1.call-update) | async-done | bytes 1048592 | tf_op jit(solution)/shard_map/all_gather | solution.py:94
  104.7 10.0 %fusion.9 = f32[4,256]{1,0:T(4,128)S(1)} fusion(bf16[4096,128]{1,0:T(8,128)(2,1)} %all-gather.4.cloned.1.call-done, bf16[256,4,128]{0,2,1:T(8,128)(2,1)} %bitcast.86, f32[4096,256,4]{1,0,2:T(8,128)} %copy-done.2, f32[4,256]{1,0:T(4,128)S(1)} %log_add_fusion, pred[256,4096]{0,1:T(8,128)(4,1)S(1)} %bitcast_and_fusion), kind=kOutput, calls=%fused_computation.21 | convolution fusion | flops 1095105536 | bytes 19144704 | tf_op jit(solution)/shard_map/gts,sd->gtd/dot_general | solution.py:45
  114.7 9.6 %fusion.2 = bf16[4,256,4096]{1,2,0:T(8,128)(2,1)S(1)} fusion(f32[4096,256,4]{1,0,2:T(8,128)} %copy-done.2, bf16[256,4,128]{0,2,1:T(8,128)(2,1)S(1)} %bitcast.88, f32[4,256]{1,0:T(4,128)S(1)} %fusion.9, f32[4,256]{1,0:T(4,128)S(1)} %log_add_fusion, pred[256,4096]{0,1:T(8,128)(4,1)S(1)} %bitcast_and_fusion, bf16[4096,128]{1,0:T(8,128)(2,1)S(1)} %copy-done.13), kind=kOutput, calls=%fused_computation.3 | convolution fusion | flops 1107296256 | bytes 27533312 | tf_op jit(solution)/shard_map/tgd,sd->gts/dot_general | solution.py:45
  124.4 3.2 copy-done.1
  127.6 3.9 fusion.7
  131.5 0.3 reduce-scatter.7.cloned.1.call-start
  131.8 11.4 %fusion.8 = bf16[4096,128]{1,0:T(8,128)(2,1)} fusion(bf16[256,4,128]{0,2,1:T(8,128)(2,1)} %bitcast.87, f32[4096,256,4]{1,0,2:T(8,128)} %copy-done.2, f32[4,256]{1,0:T(4,128)S(1)} %log_add_fusion, pred[256,4096]{0,1:T(8,128)(4,1)S(1)} %bitcast_and_fusion), kind=kOutput, calls=%fused_computation.17 | convolution fusion | flops 1095237632 | bytes 19140608 | tf_op jit(solution)/shard_map/gts,tgd->sd/dot_general | solution.py:45
  143.3 7.2 %convolution_bitcast_fusion.2 = f32[256,4,128]{2,0,1:T(8,128)S(1)} fusion(bf16[4,256,4096]{1,2,0:T(8,128)(2,1)} %copy-done.1, bf16[4096,1,128]{0,2,1:T(8,128)(2,1)} %all-gather.6.cloned.1.call-done), kind=kOutput, calls=%fused_computation.20 | convolution fusion | flops 1073741824 | bytes 9961472 | tf_op jit(solution)/shard_map/gts,sd->tgd/dot_general | solution.py:45
  150.5 0.3 subtract_convert_fusion
  150.8 0.1 pad_maximum_fusion.1
  151.1 46.3 %reduce-scatter.5.cloned.1.call-done = bf16[256,128]{0,1:T(8,128)(2,1)} async-done(((bf16[4096,128]{0,1:T(8,128)(2,1)}), bf16[256,128]{0,1:T(8,128)(2,1)}) %reduce-scatter.5.cloned.1.call-update) | async-done | bytes 65552 | tf_op jit(solution)/shard_map/reduce_scatter | solution.py:109
  197.3 0.8 bitcast_convert_fusion
  198.2 0.3 fusion.30
  198.5 68.9 %reduce-scatter.7.cloned.1.call-done = bf16[256,128]{1,0:T(8,128)(2,1)} async-done(((bf16[4096,128]{1,0:T(8,128)(2,1)}), bf16[256,128]{1,0:T(8,128)(2,1)}) %reduce-scatter.7.cloned.1.call-update) | async-done | bytes 65552 | tf_op jit(solution)/shard_map/reduce_scatter | solution.py:112
  267.5 0.9 copy.40
  268.4 4.5 %fusion.5 = bf16[4096,768]{0,1:T(8,128)(2,1)} fusion(bf16[256,4096]{1,0:T(8,128)(2,1)S(1)} %copy-done, bf16[256,128]{0,1:T(8,128)(2,1)S(1)} %copy.40, bf16[256,128]{0,1:T(8,128)(2,1)S(1)} %maximum_bitcast_fusion, bf16[256,512]{0,1:T(8,128)(2,1)S(1)} %bitcast.84), kind=kOutput, calls=%fused_computation.10 | convolution fusion | flops 1614938112 | bytes 8781824 | tf_op jit(solution)/shard_map/dot_general | solution.py:121
  272.9 0.3 reduce-scatter.9.cloned.1.call-start
  273.2 2.0 fusion.50
  275.2 3.6 convolution_add_fusion
  278.9 2.1 fusion.6
  281.0 80.8 %reduce-scatter.11.cloned.1.call-done = bf16[256,768]{0,1:T(8,128)(2,1)} async-done(((bf16[4096,768]{0,1:T(8,128)(2,1)}), bf16[256,768]{0,1:T(8,128)(2,1)}) %reduce-scatter.11.cloned.1.call-update) | async-done | bytes 393232 | tf_op jit(solution)/shard_map/reduce_scatter | solution.py:120
  361.8 1.0 slice.52
  362.8 1.0 copy.41
  363.8 0.9 fusion.54
  364.7 0.8 copy.42
  365.4 0.8 copy.43
  366.2 40.0 %reduce-scatter.9.cloned.1.call-done = bf16[256,512]{1,0:T(8,128)(2,1)} async-done(((bf16[256,4096]{1,0:T(8,128)(2,1)}), bf16[256,512]{1,0:T(8,128)(2,1)}) %reduce-scatter.9.cloned.1.call-update) | async-done | bytes 262160 | tf_op jit(solution)/shard_map/reduce_scatter | solution.py:143
  (41 shorter events, 0.7 us)
Async XLA Ops:
  7.2 1.6 copy-start
  7.2 50.2 %all-gather.6.cloned.1.call-start = ((), (), s32[]{:S(2)}) async-start(), calls=%async_computation.9 | async-start | bytes 1114112 | tf_op jit(solution)/shard_map/all_gather | solution.py:93
  7.2 9.1 %copy-start.11 = (f32[64]{0:T(128)}, f32[64]{0:T(128)S(1)}, u32[]{:S(2)}) copy-start(f32[64]{0:T(128)S(1)} %negate_power_fusion) | copy-start | bytes 772
  8.8 7.6 %copy-start.9 = (f32[256]{0:T(256)}, f32[256]{0:T(256)S(1)}, u32[]{:S(2)}) copy-start(f32[256]{0:T(256)S(1)} %convert_element_type.52) | copy-start | bytes 3076
  8.8 14.5 %copy-start.7 = (bf16[256,512]{1,0:T(8,128)(2,1)S(1)}, bf16[256,512]{1,0:T(8,128)(2,1)}, u32[]{:S(2)}) copy-start(bf16[256,512]{1,0:T(8,128)(2,1)} %param.13) | copy-start | bytes 786436
  11.9 92.9 %all-gather.4.cloned.1.call-start = ((), (), s32[]{:S(2)}) async-start(), calls=%async_computation.4 | async-start | bytes 1114112 | tf_op jit(solution)/shard_map/all_gather | solution.py:94
  14.5 182.9 %reduce-scatter.5.cloned.1.call-start = ((), (), s32[]{:S(2)}) async-start(), calls=%async_computation.5 | async-start | bytes 1114112 | tf_op jit(solution)/shard_map/reduce_scatter | solution.py:109
  61.8 5.7 %copy-start.2 = (f32[4096,256,4]{1,0,2:T(8,128)}, f32[4096,256,4]{1,0,2:T(8,128)S(1)}, u32[]{:S(2)}) copy-start(f32[4096,256,4]{1,0,2:T(8,128)S(1)} %get-tuple-element.28) | copy-start | bytes 50331652
  104.7 10.0 %copy-start.8 = (bf16[256,512]{0,1:T(8,128)(2,1)S(1)}, bf16[256,512]{0,1:T(8,128)(2,1)}, u32[]{:S(2)}) copy-start(bf16[256,512]{0,1:T(8,128)(2,1)} %copy.31) | copy-start | bytes 786436
  104.7 10.0 %copy-start.13 = (bf16[4096,128]{1,0:T(8,128)(2,1)S(1)}, bf16[4096,128]{1,0:T(8,128)(2,1)}, u32[]{:S(2)}) copy-start(bf16[4096,128]{1,0:T(8,128)(2,1)} %all-gather.4.cloned.1.call-done) | copy-start | bytes 3145732
  114.7 12.9 %copy-start.4 = (bf16[256,4,64]{2,0,1:T(8,128)(2,1)S(1)}, bf16[256,4,64]{2,0,1:T(8,128)(2,1)}, u32[]{:S(2)}) copy-start(bf16[256,4,64]{2,0,1:T(8,128)(2,1)} %get-tuple-element.13) | copy-start | bytes 393220
  124.4 3.2 copy-start.1
  131.5 135.9 %reduce-scatter.7.cloned.1.call-start = ((), (), s32[]{:S(2)}) async-start(), calls=%async_computation.6 | async-start | bytes 1114112 | tf_op jit(solution)/shard_map/reduce_scatter | solution.py:112
  143.2 7.3 %copy-start.5 = (f32[256,64]{1,0:T(8,128)S(1)}, f32[256,64]{1,0:T(8,128)}, u32[]{:S(2)}) copy-start(f32[256,64]{1,0:T(8,128)} %get-tuple-element.24) | copy-start | bytes 196612
  143.2 55.0 %copy-start.10 = (f32[256]{0:T(256)S(1)}, f32[256]{0:T(256)}, u32[]{:S(2)}) copy-start(f32[256]{0:T(256)} %copy-done.9) | copy-start | bytes 3076
  143.2 55.0 %copy-start.12 = (f32[64]{0:T(128)S(1)}, f32[64]{0:T(128)}, u32[]{:S(2)}) copy-start(f32[64]{0:T(128)} %copy-done.11) | copy-start | bytes 772
  143.2 218.6 %reduce-scatter.11.cloned.1.call-start = ((), (), s32[]{:S(2)}) async-start(), calls=%async_computation.8 | async-start | bytes 6684672 | tf_op jit(solution)/shard_map/reduce_scatter | solution.py:120
  272.9 5.9 %copy-start.3 = (bf16[4096,128]{1,0:T(8,128)(2,1)S(1)}, bf16[4096,128]{1,0:T(8,128)(2,1)}, u32[]{:S(2)}) copy-start(bf16[4096,128]{1,0:T(8,128)(2,1)} %param.10) | copy-start | bytes 3145732
  272.9 5.9 %copy-start.6 = (bf16[256,128]{1,0:T(8,128)(2,1)S(1)}, bf16[256,128]{1,0:T(8,128)(2,1)}, u32[]{:S(2)}) copy-start(bf16[256,128]{1,0:T(8,128)(2,1)} %reduce-scatter.7.cloned.1.call-done) | copy-start | bytes 196612
  272.9 133.3 %reduce-scatter.9.cloned.1.call-start = ((), (), s32[]{:S(2)}) async-start(), calls=%async_computation.7 | async-start | bytes 2359296 | tf_op jit(solution)/shard_map/reduce_scatter | solution.py:143
Sparse Core Ops, SparseCore 0:
  12.0 45.3 all-gather.5
  59.8 44.8 all-gather.3
  131.7 65.6 reduce-scatter.4
  201.4 65.9 reduce-scatter.6
  273.0 88.7 reduce-scatter.10
  364.8 41.4 reduce-scatter.8
where the time goes:
time: 414 us; the launch traced here: 413 us
  waiting for transfers between devices  302 us (73%)
  matrix products  66.8 us (16%)
  local copies, waits for them, and re-layouts  14.5 us (4%)
  other arithmetic  14.5 us (4%)
  between operations  14.4 us (3%)
    reduce_scatter x1, waiting for transfers between devices, body(): lax.psum_scatter(lax.dot_general(normed, joined, (((0,), (0,)), ((), ()))...  80.8 us
    reduce_scatter x1, waiting for transfers between devices, body(): lax.psum_scatter(grad_value.astype(jnp.bfloat16), 'seq', scatter_dimensio...  68.9 us
    dot_general x6, matrix products, product(): return jnp.einsum(form, left, right, preferred_element_type=jnp.float32)  46.6 us
    reduce_scatter x1, waiting for transfers between devices, body(): lax.psum_scatter(grad_key.astype(jnp.bfloat16), 'seq', scatter_dimension=...  46.3 us
    reduce_scatter x1, waiting for transfers between devices, body(): lax.psum_scatter(partial_input.astype(jnp.bfloat16), 'kvh', scatter_dimen...  40 us
    all_gather x1, waiting for transfers between devices, body(): lax.all_gather(values, 'seq', axis=0, tiled=True)  37.1 us
    all_gather x1, waiting for transfers between devices, body(): lax.all_gather(keys, 'seq', axis=0, tiled=True)  28.9 us
    unnamed x33, local copies, waits for them, and re-layouts  10 us
  transfers between devices with their start and end apart: 6, of which 6 were waited for; matrix products, arithmetic and copies ran while one was open for 14% of the time, Pallas kernels for 0%

commit v1 on v0

--- a/solution.py
+++ b/solution.py
@@ -76,11 +76,25 @@
     return (grad_query, grad_key, grad_value)
 
 
+def gather_rows(block, axis):
+    count = lax.axis_size(axis)
+    copies = jnp.broadcast_to(block[None], (count,) + block.shape)
+    joined = lax.all_to_all(copies, axis, 0, 0, tiled=True)
+    return joined.reshape((count * block.shape[0],) + block.shape[1:])
+
+
+def scatter_sum(parts, axis):
+    arrived = lax.all_to_all(parts, axis, 0, 0, tiled=True)
+    return jnp.sum(arrived.astype(jnp.float32), axis=0)
+
+
 def body(normed, w_query, w_key, w_value, positions, block_mask, grad_attn):
     tok_rows = normed.shape[0]
     group_size = w_query.shape[1] // w_key.shape[1]
     width_query = group_size * HEAD
     blk_local = tok_rows // BLOCK
+    seq_count = lax.axis_size("seq")
+    kvh_count = lax.axis_size("kvh")
     my_index = lax.axis_index("seq")
     queries = rotate(
         jnp.dot(normed, w_query, preferred_element_type=jnp.float32), positions, 1.0
@@ -89,60 +103,56 @@
         jnp.dot(normed, w_key, preferred_element_type=jnp.float32), positions, 1.0
     ).astype(jnp.bfloat16)
     values = jnp.dot(normed, w_value, preferred_element_type=jnp.float32).astype(jnp.bfloat16)
-    keys_all, values_all = (
-        lax.all_gather(keys, "seq", axis=0, tiled=True),
-        lax.all_gather(values, "seq", axis=0, tiled=True),
-    )
+    kv_all = gather_rows(jnp.concatenate([keys, values], axis=1), "seq")
+    keys_all = kv_all[:, :HEAD]
+    values_all = kv_all[:, HEAD:]
     seen = visible(block_mask, my_index * blk_local, tok_rows, keys_all.shape[0])
-    total_parts = []
-    dots_parts = []
     query_heads = queries.reshape(tok_rows, group_size, HEAD)
     grad_heads = grad_attn.reshape(tok_rows, group_size, HEAD)
     log_total, row_dots = softmax_stats(query_heads, keys_all, values_all, grad_heads, seen)
     grad_query, grad_key, grad_value = attention_grads(
         query_heads, keys_all, values_all, grad_heads, seen, log_total, row_dots
     )
-    query_parts = grad_query.reshape(tok_rows, width_query)
-    total_parts.append(log_total.T)
-    dots_parts.append(row_dots.T)
-    key_total, value_total = (
-        lax.psum_scatter(
-            grad_key.astype(jnp.bfloat16), "seq", scatter_dimension=0, tiled=True
-        ).astype(jnp.float32),
-        lax.psum_scatter(
-            grad_value.astype(jnp.bfloat16), "seq", scatter_dimension=0, tiled=True
-        ).astype(jnp.float32),
+    query_grad = rotate(grad_query.reshape(tok_rows, width_query), positions, -1.0).astype(
+        jnp.bfloat16
     )
-    query_grad = rotate(query_parts, positions, -1.0).astype(jnp.bfloat16)
-    key_grad = rotate(key_total, positions, -1.0).astype(jnp.bfloat16)
-    value_grad = value_total.astype(jnp.bfloat16)
-    joined = jnp.concatenate([query_grad, key_grad, value_grad], axis=1)
-    weight_grads = lax.psum_scatter(
-        lax.dot_general(
-            normed, joined, (((0,), (0,)), ((), ())), preferred_element_type=jnp.float32
-        ).astype(jnp.bfloat16),
+    kv_terms = jnp.concatenate([grad_key, grad_value], axis=1).astype(jnp.bfloat16)
+    kv_total = scatter_sum(kv_terms.reshape(seq_count, tok_rows, 2 * HEAD), "seq")
+    tokens_first = (((0,), (0,)), ((), ()))
+    grad_wq = lax.psum_scatter(
+        lax.dot_general(normed, query_grad, tokens_first, preferred_element_type=jnp.float32).astype(
+            jnp.bfloat16
+        ),
         "seq",
         scatter_dimension=0,
         tiled=True,
     ).astype(jnp.float32)
-    query_cols = query_grad.shape[1]
-    key_cols = key_grad.shape[1]
-    grad_wq = weight_grads[:, :query_cols]
-    grad_wk = weight_grads[:, query_cols : query_cols + key_cols]
-    grad_wv = weight_grads[:, query_cols + key_cols :]
     contract = (((1,), (1,)), ((), ()))
     partial_input = lax.dot_general(
         query_grad, w_query, contract, preferred_element_type=jnp.float32
     )
+    key_grad = rotate(kv_total[:, :HEAD], positions, -1.0).astype(jnp.bfloat16)
+    value_grad = kv_total[:, HEAD:].astype(jnp.bfloat16)
+    kv_grad = jnp.concatenate([key_grad, value_grad], axis=1)
+    grad_wkv = lax.psum_scatter(
+        lax.dot_general(normed, kv_grad, tokens_first, preferred_element_type=jnp.float32).astype(
+            jnp.bfloat16
+        ),
+        "seq",
+        scatter_dimension=0,
+        tiled=True,
+    ).astype(jnp.float32)
+    grad_wk = grad_wkv[:, :HEAD]
+    grad_wv = grad_wkv[:, HEAD:]
     partial_input = partial_input + lax.dot_general(
         key_grad, w_key, contract, preferred_element_type=jnp.float32
     )
     partial_input = partial_input + lax.dot_general(
         value_grad, w_value, contract, preferred_element_type=jnp.float32
     )
-    grad_normed = lax.psum_scatter(
-        partial_input.astype(jnp.bfloat16), "kvh", scatter_dimension=1, tiled=True
-    )
+    feat = partial_input.shape[1] // kvh_count
+    input_terms = partial_input.astype(jnp.bfloat16).reshape(tok_rows, kvh_count, feat)
+    grad_normed = scatter_sum(jnp.transpose(input_terms, (1, 0, 2)), "kvh").astype(jnp.bfloat16)
     return (grad_normed, grad_wq, grad_wk, grad_wv)
 
 

time: 414 us -> 300 us (0.72)
  waiting for transfers between devices: 302 us -> 120 us
  blocking collectives: 0 us -> 71.7 us
  matrix products: 66.8 us -> 52 us
  starting transfers between devices: 0.73 us -> 8.1 us
    reduce_scatter x4 -> x2, waiting for transfers between devices: 236 us -> 101 us  [the longest x1 81.8 us: body(): lax.psum_scatter(lax.dot_general(normed, query_grad, tokens_first, prefer...]
    all_to_all x0 -> x2, blocking collectives: none -> 71.7 us  [scatter_sum(): arrived = lax.all_to_all(parts, axis, 0, 0, tiled=True)]
    all_gather x2 -> x0, waiting for transfers between devices: 66 us -> none  [the longest x1 37.1 us: body(): lax.all_gather(values, 'seq', axis=0, tiled=True)]
    all_to_all x0 -> x1, waiting for transfers between devices: none -> 19.1 us  [gather_rows(): joined = lax.all_to_all(copies, axis, 0, 0, tiled=True)]
    dot_general x6, matrix products: 46.6 us -> 36.4 us  [product(): return jnp.einsum(form, left, right, preferred_element_type=jnp.float32)]
    all_to_all x0 -> x1, starting transfers between devices: none -> 8.02 us  [gather_rows(): joined = lax.all_to_all(copies, axis, 0, 0, tiled=True)]
    convert_element_type x1 -> x3, other arithmetic: 0.01 us -> 6.2 us  [the longest x1 6.18 us: softmax_stats(): jnp.where(seen[None], jnp.exp(scores - log_total[:, :, None]), 0.0)]
    unnamed x33 -> x31, local copies, waits for them, and re-layouts: 10 us -> 7.32 us
  transfers between devices with their start and end apart: 6 -> 3, of which waited for: 6 -> 3; matrix products, arithmetic and copies ran while one was open for 14% -> 10% of each run, Pallas kernels for 0% -> 0%
where the time goes in v1:
time: 300 us; the launch traced here: 299 us
  waiting for transfers between devices  120 us (40%)
  blocking collectives  71.7 us (24%)
  matrix products  52 us (17%)
  other arithmetic  18 us (6%)
  local copies, waits for them, and re-layouts  14.4 us (5%)
  between operations  14.4 us (5%)
  starting transfers between devices  8.1 us (3%)
    reduce_scatter x1, waiting for transfers between devices, body(): lax.psum_scatter(lax.dot_general(normed, query_grad, tokens_first, prefer...  81.8 us
    all_to_all x2, blocking collectives, scatter_sum(): arrived = lax.all_to_all(parts, axis, 0, 0, tiled=True)  71.7 us
    dot_general x6, matrix products, product(): return jnp.einsum(form, left, right, preferred_element_type=jnp.float32)  36.4 us
    reduce_scatter x1, waiting for transfers between devices, body(): lax.psum_scatter(lax.dot_general(normed, kv_grad, tokens_first, preferred...  19.5 us
    all_to_all x1, waiting for transfers between devices, gather_rows(): joined = lax.all_to_all(copies, axis, 0, 0, tiled=True)  19.1 us
    all_to_all x1, starting transfers between devices, gather_rows(): joined = lax.all_to_all(copies, axis, 0, 0, tiled=True)  8.02 us
    unnamed x31, local copies, waits for them, and re-layouts  7.32 us
    convert_element_type x1, other arithmetic, softmax_stats(): jnp.where(seen[None], jnp.exp(scores - log_total[:, :, None]), 0.0)  6.18 us
  transfers between devices with their start and end apart: 3, of which 3 were waited for; matrix products, arithmetic and copies ran while one was open for 10% of the time, Pallas kernels for 0%

profile of v1, /device:TPU:0, one launch (start us, length us, event | category | flops | bytes accessed | tf_op | source)
XLA Modules:
  0.0 299.0 jit_solution(194471450990499321)
XLA Ops:
  7.2 0.8 convert_element_type.63
  8.0 0.8 copy-done
  8.8 2.0 convolution_convert_fusion.2
  10.8 2.0 convolution_bitcast_fusion.2
  12.9 0.3 fusion.39
  13.4 1.5 broadcast_in_dim.76
  14.9 8.0 %all-to-all-start = ((bf16[16,256,256]{2,1,0:T(8,128)(2,1)}), bf16[16,256,256]{2,1,0:T(8,128)(2,1)}, u32[]{:S(2)}, u32[]{:S(2)}) async-start(bf16[16,256,256]{2,1,0:T(8,128)(2,1)} %broadcast_in_dim.76), calls=%async_computation | async-start | bytes 4194304 | tf_op jit(solution)/shard_map/all_to_all | solution.py:82
  23.0 0.1 copy.45
  23.2 3.5 %fusion.62 = f32[256,512]{1,0:T(8,128)S(1)} fusion(bf16[256,4096]{1,0:T(8,128)(2,1)S(1)} %copy-done, bf16[4096,512]{1,0:T(8,128)(2,1)} %param.8), kind=kOutput, calls=%fused_computation.106 | convolution fusion | flops 1073741824 | bytes 6815744 | tf_op jit(solution)/shard_map/dot_general | solution.py:100
  26.7 1.0 reshape.303
  27.7 0.9 copy.48
  28.6 1.6 bitcast_and_fusion
  30.2 0.5 broadcast_multiply_fusion
  30.7 1.6 fusion.59
  32.3 0.9 subtract_convert_fusion.1
  33.2 19.1 %all-to-all-done = bf16[16,256,256]{2,1,0:T(8,128)(2,1)} async-done(((bf16[16,256,256]{2,1,0:T(8,128)(2,1)}), bf16[16,256,256]{2,1,0:T(8,128)(2,1)}, u32[]{:S(2)}, u32[]{:S(2)}) %all-to-all-start) | async-done | bytes 2097184 | tf_op jit(solution)/shard_map/all_to_all | solution.py:82
  52.3 4.3 %fusion.7 = (f32[4,256]{1,0:T(4,128)S(1)}, f32[4096,256,4]{1,0,2:T(8,128)S(1)}) fusion(pred[256,4096]{0,1:T(8,128)(4,1)S(1)} %bitcast_and_fusion, bf16[256,4,64]{2,0,1:T(8,128)(2,1)} %get-tuple-element.17, bf16[256,4,64]{2,0,1:T(8,128)(2,1)} %get-tuple-element.16, bf16[4096,256]{1,0:T(8,128)(2,1)} %bitcast.2), kind=kOutput, calls=%fused_computation.12 | convolution fusion | flops 1086848000 | bytes 19402752 | tf_op jit(solution)/shard_map/tgd,sd->gts/dot_general | solution.py:45
  56.6 3.7 %exponential_reduce_fusion = f32[4,256]{1,0:T(4,128)S(1)} fusion(f32[4096,256,4]{1,0,2:T(8,128)S(1)} %get-tuple-element.32, f32[4,256]{1,0:T(4,128)S(1)} %get-tuple-element.31, pred[256,4096]{0,1:T(8,128)(4,1)S(1)} %bitcast_and_fusion), kind=kLoop, calls=%fused_computation.10 | loop fusion | flops 16776192 | bytes 17833984 | tf_op jit(solution)/shard_map/reduce_sum | solution.py:56
  60.3 6.2 %fusion.2 = bf16[4096,4,256]{2,0,1:T(8,128)(2,1)} fusion(f32[4096,256,4]{1,0,2:T(8,128)S(1)} %get-tuple-element.32, f32[4,256]{1,0:T(4,128)S(1)} %log_add_fusion, pred[4096,256]{1,0:T(8,128)(4,1)S(1)} %bitcast.109), kind=kLoop, calls=%fused_computation.3 | loop fusion | flops 20971520 | bytes 26218496 | tf_op jit(solution)/shard_map/convert_element_type | solution.py:57
  66.5 5.1 %fusion.18 = f32[4,256]{1,0:T(4,128)S(1)} fusion(f32[4096,256,4]{1,0,2:T(8,128)S(1)} %get-tuple-element.32, f32[4,256]{1,0:T(4,128)S(1)} %log_add_fusion, pred[256,4096]{0,1:T(8,128)(4,1)S(1)} %bitcast_and_fusion, bf16[4096,256]{1,0:T(8,128)(2,1)} %bitcast.2, bf16[256,4,128]{0,2,1:T(8,128)(2,1)S(1)} %bitcast.117), kind=kOutput, calls=%fused_computation.31 | convolution fusion | flops 1095105536 | bytes 19144704 | tf_op jit(solution)/shard_map/gts,sd->gtd/dot_general | solution.py:45
  71.6 10.0 %fusion.5 = bf16[4,256,4096]{1,2,0:T(8,128)(2,1)S(1)} fusion(f32[4096,256,4]{1,0,2:T(8,128)} %copy-done.1, bf16[256,4,128]{0,2,1:T(8,128)(2,1)S(1)} %bitcast.118, f32[4,256]{1,0:T(4,128)S(1)} %fusion.18, f32[4,256]{1,0:T(4,128)S(1)} %log_add_fusion, pred[256,4096]{0,1:T(8,128)(4,1)S(1)} %bitcast_and_fusion, bf16[4096,256]{1,0:T(8,128)(2,1)} %bitcast.2), kind=kOutput, calls=%fused_computation.7 | convolution fusion | flops 1107296256 | bytes 27533312 | tf_op jit(solution)/shard_map/tgd,sd->gts/dot_general | solution.py:45
  81.7 3.6 %fusion.14 = bf16[4096,128]{1,0:T(8,128)(2,1)} fusion(bf16[4,256,4096]{1,2,0:T(8,128)(2,1)S(1)} %fusion.5, bf16[256,4,64]{2,0,1:T(8,128)(2,1)S(1)} %copy-done.9, bf16[256,4,64]{2,0,1:T(8,128)(2,1)S(1)} %copy-done.8), kind=kOutput, calls=%fused_computation.23 | convolution fusion | flops 1074790400 | bytes 9699328 | tf_op jit(solution)/shard_map/gts,tgd->sd/dot_general | solution.py:45
  85.3 1.5 copy.56
  86.8 6.2 %bitcast_convert_fusion = bf16[16,256,128]{1,2,0:T(8,128)(2,1)S(1)} fusion(bf16[16,256,4,256]{3,1,0,2:T(8,128)(2,1)} %bitcast.111, bf16[256,4,128,1]{0,2,3,1:T(8,128)(2,1)} %bitcast.116), kind=kOutput, calls=%fused_computation.28 | convolution fusion | flops 1074266112 | bytes 9699328 | tf_op jit(solution)/shard_map/gts,tgd->sd/dot_general | solution.py:45
  93.0 0.2 pad_maximum_fusion
  93.2 35.3 %all_to_all.15 = bf16[16,256,256]{1,2,0:T(8,128)(2,1)S(1)} all-to-all(bf16[16,256,256]{1,2,0:T(8,128)(2,1)S(1)} %pad_maximum_fusion), channel_id=1, replica_groups=mesh['seq'=16,'kvh'=8] {'seq'}, dimensions={0} | all-to-all | bytes 4194304 | tf_op jit(solution)/shard_map/all_to_all | solution.py:87
  128.5 0.3 convert_reduce_fusion
  128.8 0.7 copy-done.6
  129.5 0.3 fusion.35
  129.9 2.1 fusion.13
  132.0 7.1 %convolution_bitcast_fusion.1 = f32[256,4,128]{2,0,1:T(8,128)S(1)} fusion(bf16[4,256,4096]{1,2,0:T(8,128)(2,1)} %copy-done.2, bf16[4096,256]{1,0:T(8,128)(2,1)} %bitcast.2), kind=kOutput, calls=%fused_computation.29 | convolution fusion | flops 1073741824 | bytes 9961472 | tf_op jit(solution)/shard_map/gts,sd->tgd/dot_general | solution.py:45
  139.1 0.3 subtract_convert_fusion
  139.4 0.1 pad_maximum_fusion.2
  139.5 0.1 copy.55
  139.7 3.2 %fusion.11 = bf16[4096,512]{0,1:T(8,128)(2,1)} fusion(bf16[256,512]{0,1:T(8,128)(2,1)S(1)} %bitcast.113, bf16[256,4096]{1,0:T(8,128)(2,1)S(1)} %copy-done), kind=kOutput, calls=%fused_computation.16 | convolution fusion | flops 1075838976 | bytes 6553600 | tf_op jit(solution)/shard_map/dot_general | solution.py:123
  142.9 0.7 fusion.58
  143.7 1.6 copy-done.3
  145.3 1.3 convolution_add_fusion
  146.6 0.7 fusion.12
  147.4 0.2 copy.80
  147.6 36.4 %all_to_all.16 = bf16[8,256,512]{2,1,0:T(8,128)(2,1)} all-to-all(bf16[8,256,512]{2,1,0:T(8,128)(2,1)S(1)} %bitcast.112), channel_id=1, replica_groups=mesh['seq'=16,'kvh'=8] {'kvh'}, dimensions={0} | all-to-all | bytes 4194304 | tf_op jit(solution)/shard_map/all_to_all | solution.py:87
  184.0 2.7 reduce_sum.42
  186.6 19.5 %reduce-scatter.5.cloned.1.call-done = bf16[256,256]{0,1:T(8,128)(2,1)} async-done(((bf16[4096,256]{0,1:T(8,128)(2,1)}), bf16[256,256]{0,1:T(8,128)(2,1)}) %reduce-scatter.5.cloned.1.call-update) | async-done | bytes 131088 | tf_op jit(solution)/shard_map/reduce_scatter | solution.py:137
  206.1 0.9 fusion.60
  207.0 0.8 copy.59
  207.8 0.8 copy.60
  208.5 81.8 %reduce-scatter.3.cloned.1.call-done = bf16[256,512]{0,1:T(8,128)(2,1)} async-done(((bf16[4096,512]{0,1:T(8,128)(2,1)}), bf16[256,512]{0,1:T(8,128)(2,1)}) %reduce-scatter.3.cloned.1.call-update) | async-done | bytes 262160 | tf_op jit(solution)/shard_map/reduce_scatter | solution.py:122
  290.3 1.9 copy.58
  (40 shorter events, 0.5 us)
Async XLA Ops:
  7.2 1.6 copy-start
  12.9 10.1 %copy-start.12 = (s32[2,32]{1,0:T(2,128)S(1)}, s32[2,32]{1,0:T(2,128)}, u32[]{:S(2)}) copy-start(s32[2,32]{1,0:T(2,128)} %param.12) | copy-start | bytes 772
  14.9 37.4 %all-to-all-start = ((bf16[16,256,256]{2,1,0:T(8,128)(2,1)}), bf16[16,256,256]{2,1,0:T(8,128)(2,1)}, u32[]{:S(2)}, u32[]{:S(2)}) async-start(bf16[16,256,256]{2,1,0:T(8,128)(2,1)} %broadcast_in_dim.76), calls=%async_computation | async-start | bytes 4194304 | tf_op jit(solution)/shard_map/all_to_all | solution.py:82
  22.9 183.2 %reduce-scatter.5.cloned.1.call-start = ((), (), s32[]{:S(2)}) async-start(), calls=%async_computation.6 | async-start | bytes 2228224 | tf_op jit(solution)/shard_map/reduce_scatter | solution.py:137
  23.2 4.5 %copy-start.10 = (bf16[256,512]{1,0:T(8,128)(2,1)S(1)}, bf16[256,512]{1,0:T(8,128)(2,1)}, u32[]{:S(2)}) copy-start(bf16[256,512]{1,0:T(8,128)(2,1)} %param.13) | copy-start | bytes 786436
  56.6 9.9 %copy-start.1 = (f32[4096,256,4]{1,0,2:T(8,128)}, f32[4096,256,4]{1,0,2:T(8,128)S(1)}, u32[]{:S(2)}) copy-start(f32[4096,256,4]{1,0,2:T(8,128)S(1)} %get-tuple-element.32) | copy-start | bytes 50331652
  60.3 6.2 %copy-start.11 = (bf16[256,512]{0,1:T(8,128)(2,1)S(1)}, bf16[256,512]{0,1:T(8,128)(2,1)}, u32[]{:S(2)}) copy-start(bf16[256,512]{0,1:T(8,128)(2,1)} %copy.48) | copy-start | bytes 786436
  71.6 10.1 %copy-start.8 = (bf16[256,4,64]{2,0,1:T(8,128)(2,1)S(1)}, bf16[256,4,64]{2,0,1:T(8,128)(2,1)}, u32[]{:S(2)}) copy-start(bf16[256,4,64]{2,0,1:T(8,128)(2,1)} %get-tuple-element.16) | copy-start | bytes 393220
  71.6 10.1 %copy-start.9 = (bf16[256,4,64]{2,0,1:T(8,128)(2,1)S(1)}, bf16[256,4,64]{2,0,1:T(8,128)(2,1)}, u32[]{:S(2)}) copy-start(bf16[256,4,64]{2,0,1:T(8,128)(2,1)} %get-tuple-element.17) | copy-start | bytes 393220
  81.7 3.6 %copy-start.2 = (bf16[4,256,4096]{1,2,0:T(8,128)(2,1)}, bf16[4,256,4096]{1,2,0:T(8,128)(2,1)S(1)}, u32[]{:S(2)}) copy-start(bf16[4,256,4096]{1,2,0:T(8,128)(2,1)S(1)} %fusion.5) | copy-start | bytes 25165828
  128.8 0.7 copy-start.6
  132.0 158.3 %reduce-scatter.3.cloned.1.call-start = ((), (), s32[]{:S(2)}) async-start(), calls=%async_computation.5 | async-start | bytes 4456448 | tf_op jit(solution)/shard_map/reduce_scatter | solution.py:122
  139.7 3.2 %copy-start.5 = (bf16[4096,128]{1,0:T(8,128)(2,1)S(1)}, bf16[4096,128]{1,0:T(8,128)(2,1)}, u32[]{:S(2)}) copy-start(bf16[4096,128]{1,0:T(8,128)(2,1)} %param.9) | copy-start | bytes 3145732
  142.9 2.3 copy-start.3
  145.3 1.4 copy-start.4
  145.3 1.4 copy-start.7
Sparse Core Ops, SparseCore 0:
  132.1 73.9 reduce-scatter.4
  210.7 79.5 reduce-scatter.2

commit v2 on v1

--- a/solution.py
+++ b/solution.py
@@ -76,11 +76,37 @@
     return (grad_query, grad_key, grad_value)
 
 
-def gather_rows(block, axis):
-    count = lax.axis_size(axis)
-    copies = jnp.broadcast_to(block[None], (count,) + block.shape)
-    joined = lax.all_to_all(copies, axis, 0, 0, tiled=True)
-    return joined.reshape((count * block.shape[0],) + block.shape[1:])
+SEQ_AXES = ("seq_x", "seq_z", "seq_core")
+KVH_AXES = ("kvh_x", "kvh_y")
+PAIR = [(0, 1), (1, 0)]
+
+
+def seq_position():
+    return (lax.axis_index("seq_x") * lax.axis_size("seq_z") + lax.axis_index("seq_z")) * 2 + lax.axis_index(
+        "seq_core"
+    )
+
+
+def gather_rows(block):
+    chips = lax.axis_size("seq_x") * lax.axis_size("seq_z")
+    copies = jnp.broadcast_to(block[None], (chips,) + block.shape)
+    mine = lax.all_to_all(copies, ("seq_x", "seq_z"), 0, 0, tiled=True)
+    other = lax.ppermute(mine, "seq_core", PAIR)
+    first = lax.axis_index("seq_core") == 0
+    low = jnp.where(first, mine, other)
+    high = jnp.where(first, other, mine)
+    joined = jnp.stack([low, high], axis=1)
+    return joined.reshape((chips * 2 * block.shape[0],) + block.shape[1:])
+
+
+def pair_reduce(terms):
+    chips = lax.axis_size("seq_x") * lax.axis_size("seq_z")
+    split = terms.reshape((chips, 2, terms.shape[0] // (2 * chips)) + terms.shape[1:])
+    core = lax.axis_index("seq_core")
+    keep = lax.dynamic_index_in_dim(split, core, axis=1, keepdims=False)
+    send = lax.dynamic_index_in_dim(split, 1 - core, axis=1, keepdims=False)
+    got = lax.ppermute(send, "seq_core", PAIR)
+    return (keep.astype(jnp.float32) + got.astype(jnp.float32)).astype(jnp.bfloat16)
 
 
 def scatter_sum(parts, axis):
@@ -93,9 +119,8 @@
     group_size = w_query.shape[1] // w_key.shape[1]
     width_query = group_size * HEAD
     blk_local = tok_rows // BLOCK
-    seq_count = lax.axis_size("seq")
-    kvh_count = lax.axis_size("kvh")
-    my_index = lax.axis_index("seq")
+    kvh_count = lax.axis_size("kvh_x") * lax.axis_size("kvh_y")
+    my_index = seq_position()
     queries = rotate(
         jnp.dot(normed, w_query, preferred_element_type=jnp.float32), positions, 1.0
     ).astype(jnp.bfloat16)
@@ -103,7 +128,7 @@
         jnp.dot(normed, w_key, preferred_element_type=jnp.float32), positions, 1.0
     ).astype(jnp.bfloat16)
     values = jnp.dot(normed, w_value, preferred_element_type=jnp.float32).astype(jnp.bfloat16)
-    kv_all = gather_rows(jnp.concatenate([keys, values], axis=1), "seq")
+    kv_all = gather_rows(jnp.concatenate([keys, values], axis=1))
     keys_all = kv_all[:, :HEAD]
     values_all = kv_all[:, HEAD:]
     seen = visible(block_mask, my_index * blk_local, tok_rows, keys_all.shape[0])
@@ -117,13 +142,16 @@
         jnp.bfloat16
     )
     kv_terms = jnp.concatenate([grad_key, grad_value], axis=1).astype(jnp.bfloat16)
-    kv_total = scatter_sum(kv_terms.reshape(seq_count, tok_rows, 2 * HEAD), "seq")
+    kv_total = scatter_sum(pair_reduce(kv_terms), ("seq_x", "seq_z"))
     tokens_first = (((0,), (0,)), ((), ()))
-    grad_wq = lax.psum_scatter(
+    wq_terms = pair_reduce(
         lax.dot_general(normed, query_grad, tokens_first, preferred_element_type=jnp.float32).astype(
             jnp.bfloat16
-        ),
-        "seq",
+        )
+    )
+    grad_wq = lax.psum_scatter(
+        wq_terms.reshape((-1,) + wq_terms.shape[2:]),
+        ("seq_x", "seq_z"),
         scatter_dimension=0,
         tiled=True,
     ).astype(jnp.float32)
@@ -134,14 +162,12 @@
     key_grad = rotate(kv_total[:, :HEAD], positions, -1.0).astype(jnp.bfloat16)
     value_grad = kv_total[:, HEAD:].astype(jnp.bfloat16)
     kv_grad = jnp.concatenate([key_grad, value_grad], axis=1)
-    grad_wkv = lax.psum_scatter(
+    wkv_terms = pair_reduce(
         lax.dot_general(normed, kv_grad, tokens_first, preferred_element_type=jnp.float32).astype(
             jnp.bfloat16
-        ),
-        "seq",
-        scatter_dimension=0,
-        tiled=True,
-    ).astype(jnp.float32)
+        )
+    )
+    grad_wkv = scatter_sum(wkv_terms, ("seq_x", "seq_z"))
     grad_wk = grad_wkv[:, :HEAD]
     grad_wv = grad_wkv[:, HEAD:]
     partial_input = partial_input + lax.dot_general(
@@ -152,19 +178,24 @@
     )
     feat = partial_input.shape[1] // kvh_count
     input_terms = partial_input.astype(jnp.bfloat16).reshape(tok_rows, kvh_count, feat)
-    grad_normed = scatter_sum(jnp.transpose(input_terms, (1, 0, 2)), "kvh").astype(jnp.bfloat16)
+    grad_normed = scatter_sum(jnp.transpose(input_terms, (1, 0, 2)), KVH_AXES).astype(jnp.bfloat16)
     return (grad_normed, grad_wq, grad_wk, grad_wv)
 
 
 def solution(mesh):
+    seq_x = 2
+    seq_size = mesh.shape["seq"]
+    kvh_size = mesh.shape["kvh"]
+    grid = mesh.devices.reshape(seq_x, seq_size // (2 * seq_x), 2, 2, kvh_size // 2)
+    fine = jax.sharding.Mesh(grid, SEQ_AXES + KVH_AXES)
     in_specs = (
-        P("seq", None),
-        P(None, "kvh"),
-        P(None, "kvh"),
-        P(None, "kvh"),
-        P("seq"),
-        P("seq", None),
-        P("seq", "kvh"),
-    )
-    out_specs = (P("seq", "kvh"), P("seq", "kvh"), P("seq", "kvh"), P("seq", "kvh"))
-    return jax.shard_map(body, mesh=mesh, in_specs=in_specs, out_specs=out_specs, check_vma=False)
+        P(SEQ_AXES, None),
+        P(None, KVH_AXES),
+        P(None, KVH_AXES),
+        P(None, KVH_AXES),
+        P(SEQ_AXES),
+        P(SEQ_AXES, None),
+        P(SEQ_AXES, KVH_AXES),
+    )
+    out_specs = (P(SEQ_AXES, KVH_AXES),) * 4
+    return jax.shard_map(body, mesh=fine, in_specs=in_specs, out_specs=out_specs, check_vma=False)

time: 300 us -> 259 us (0.86); the launches traced: 299 us -> 254 us
  waiting for transfers between devices: 120 us -> 45.5 us
  blocking collectives: 71.7 us -> 0 us
  local copies, waits for them, and re-layouts: 14.4 us -> 76.1 us
  starting transfers between devices: 8.1 us -> 24.3 us
  other arithmetic: 18 us -> 32.1 us
  matrix products: 52 us -> 61.5 us
    reduce_scatter x2 -> x1, waiting for transfers between devices: 101 us -> 13.2 us  [body(): lax.psum_scatter(wq_terms.reshape((-1,) + wq_terms.shape[2:]), ('seq_x',...]
    all_to_all x2 -> x0, blocking collectives: 71.7 us -> none  [scatter_sum(): arrived = lax.all_to_all(parts, axis, 0, 0, tiled=True)]
    unnamed x31 -> x44, local copies, waits for them, and re-layouts: 7.32 us -> 36 us
    dynamic_slice x0 -> x2, local copies, waits for them, and re-layouts: none -> 20 us  [pair_reduce(): keep = lax.dynamic_index_in_dim(split, core, axis=1, keepdims=False)]
    all_to_all x1 -> x4, starting transfers between devices: 8.02 us -> 23.2 us  [the longest x3 15.4 us: scatter_sum(): arrived = lax.all_to_all(parts, axis, 0, 0, tiled=True)]
    all_to_all x1 -> x4, waiting for transfers between devices: 19.1 us -> 32.2 us  [the longest x3 19.8 us: scatter_sum(): arrived = lax.all_to_all(parts, axis, 0, 0, tiled=True)]
    reshape x0 -> x2, local copies, waits for them, and re-layouts: none -> 12.7 us  [pair_reduce(): terms.reshape((chips, 2, terms.shape[0] // (2 * chips)) + terms.shape[1:])]
    convert_element_type x0 -> x4, other arithmetic: none -> 10.4 us  [the longest x3 8.59 us: pair_reduce(): (keep.astype(jnp.float32) + got.astype(jnp.float32)).astype(jnp.bfloat16)]
  transfers between devices with their start and end apart: 3 -> 9, of which waited for: 3 -> 5; matrix products, arithmetic and copies ran while one was open for 10% -> 40% of each run, Pallas kernels for 0% -> 0%
where the time goes in v2:
time: 259 us; the launch traced here: 254 us
  local copies, waits for them, and re-layouts  76.1 us (29%)
  matrix products  61.5 us (24%)
  waiting for transfers between devices  45.5 us (18%)
  other arithmetic  32.1 us (12%)
  starting transfers between devices  24.3 us (9%)
  between operations  14.7 us (6%)
    dot_general x6, matrix products, product(): return jnp.einsum(form, left, right, preferred_element_type=jnp.float32)  39.1 us
    unnamed x44, local copies, waits for them, and re-layouts  36 us
    dynamic_slice x2, local copies, waits for them, and re-layouts, pair_reduce(): keep = lax.dynamic_index_in_dim(split, core, axis=1, keepdims=False)  20 us
    all_to_all x3, waiting for transfers between devices, scatter_sum(): arrived = lax.all_to_all(parts, axis, 0, 0, tiled=True)  19.8 us
    all_to_all x3, starting transfers between devices, scatter_sum(): arrived = lax.all_to_all(parts, axis, 0, 0, tiled=True)  15.4 us
    reduce_scatter x1, waiting for transfers between devices, body(): lax.psum_scatter(wq_terms.reshape((-1,) + wq_terms.shape[2:]), ('seq_x',...  13.2 us
    reshape x2, local copies, waits for them, and re-layouts, pair_reduce(): terms.reshape((chips, 2, terms.shape[0] // (2 * chips)) + terms.shape[1:])  12.7 us
    all_to_all x1, waiting for transfers between devices, gather_rows(): mine = lax.all_to_all(copies, ('seq_x', 'seq_z'), 0, 0, tiled=True)  12.5 us
  transfers between devices with their start and end apart: 9, of which 5 were waited for; matrix products, arithmetic and copies ran while one was open for 40% of the time, Pallas kernels for 0%

profile of v2, /device:TPU:0, one launch (start us, length us, event | category | flops | bytes accessed | tf_op | source)
XLA Modules:
  0.0 254.2 jit_solution(16744476552102429659)
XLA Ops:
  8.8 2.0 convolution_bitcast_fusion.2
  10.8 2.1 convolution_convert_fusion.2
  13.4 1.0 broadcast_in_dim.76
  14.4 7.9 %all-to-all-start = ((bf16[8,256,256]{2,1,0:T(8,128)(2,1)}), bf16[8,256,256]{2,1,0:T(8,128)(2,1)}, u32[]{:S(2)}, u32[]{:S(2)}) async-start(bf16[8,256,256]{2,1,0:T(8,128)(2,1)} %broadcast_in_dim.76), calls=%async_computation | async-start | bytes 2097152 | tf_op jit(solution)/shard_map/all_to_all | solution.py:93
  22.3 3.5 %fusion.69 = f32[256,512]{1,0:T(8,128)S(1)} fusion(bf16[256,4096]{1,0:T(8,128)(2,1)S(1)} %copy-done, bf16[4096,512]{1,0:T(8,128)(2,1)} %param.8), kind=kOutput, calls=%fused_computation.127 | convolution fusion | flops 1073741824 | bytes 6815744 | tf_op jit(solution)/shard_map/dot_general | solution.py:125
  25.7 12.5 %all-to-all-done = bf16[8,256,256]{2,1,0:T(8,128)(2,1)} async-done(((bf16[8,256,256]{2,1,0:T(8,128)(2,1)}), bf16[8,256,256]{2,1,0:T(8,128)(2,1)}, u32[]{:S(2)}, u32[]{:S(2)}) %all-to-all-start) | async-done | bytes 1048608 | tf_op jit(solution)/shard_map/all_to_all | solution.py:93
  40.0 1.4 bitcast_and_fusion
  41.5 1.2 broadcast_multiply_fusion
  43.3 1.9 select_bitcast_fusion.1
  45.4 3.0 %fusion.7 = (f32[4,256]{1,0:T(4,128)S(1)}, f32[4096,256,4]{1,0,2:T(8,128)S(1)}) fusion(pred[256,4096]{0,1:T(8,128)(4,1)S(1)} %bitcast_and_fusion, bf16[256,4,64]{2,0,1:T(8,128)(2,1)S(1)} %get-tuple-element.11, bf16[256,4,64]{2,0,1:T(8,128)(2,1)S(1)} %get-tuple-element.10, bf16[4096,256]{1,0:T(8,128)(2,1)S(1)} %bitcast.145), kind=kOutput, calls=%fused_computation.12 | convolution fusion | flops 1086848000 | bytes 19402752 | tf_op jit(solution)/shard_map/tgd,sd->gts/dot_general | solution.py:45
  48.4 3.7 %exponential_reduce_fusion = f32[4,256]{1,0:T(4,128)S(1)} fusion(f32[4096,256,4]{1,0,2:T(8,128)S(1)} %get-tuple-element.26, f32[4,256]{1,0:T(4,128)S(1)} %get-tuple-element.25, pred[256,4096]{0,1:T(8,128)(4,1)S(1)} %bitcast_and_fusion), kind=kLoop, calls=%fused_computation.10 | loop fusion | flops 16776192 | bytes 17833984 | tf_op jit(solution)/shard_map/reduce_sum | solution.py:56
  52.1 2.0 copy-done.1
  54.1 4.5 %fusion.21 = f32[4,256]{1,0:T(4,128)} fusion(f32[4096,256,4]{1,0,2:T(8,128)S(1)} %get-tuple-element.26, f32[4,256]{1,0:T(4,128)S(1)} %log_add_fusion, pred[256,4096]{0,1:T(8,128)(4,1)S(1)} %bitcast_and_fusion, bf16[4096,256]{1,0:T(8,128)(2,1)S(1)} %bitcast.146, bf16[256,4,128]{0,2,1:T(8,128)(2,1)S(1)} %bitcast.154), kind=kOutput, calls=%fused_computation.42 | convolution fusion | flops 1095105536 | bytes 19144704 | tf_op jit(solution)/shard_map/gts,sd->gtd/dot_general | solution.py:45
  58.6 14.2 %fusion.5 = bf16[4,256,4096]{1,2,0:T(8,128)(2,1)} fusion(f32[4096,256,4]{1,0,2:T(8,128)} %copy-done.1, bf16[256,4,128]{0,2,1:T(8,128)(2,1)} %bitcast.153, f32[4,256]{1,0:T(4,128)} %fusion.21, f32[4,256]{1,0:T(4,128)S(1)} %log_add_fusion, pred[256,4096]{0,1:T(8,128)(4,1)S(1)} %bitcast_and_fusion, bf16[4096,256]{1,0:T(8,128)(2,1)S(1)} %bitcast.147), kind=kOutput, calls=%fused_computation.7 | convolution fusion | flops 1107296256 | bytes 27533312 | tf_op jit(solution)/shard_map/tgd,sd->gts/dot_general | solution.py:45
  72.8 7.1 %fusion.14 = bf16[4096,128]{1,0:T(8,128)(2,1)} fusion(bf16[4,256,4096]{1,2,0:T(8,128)(2,1)} %fusion.5, bf16[256,4,64]{2,0,1:T(8,128)(2,1)} %copy-done.10, bf16[256,4,64]{2,0,1:T(8,128)(2,1)} %copy-done.9), kind=kOutput, calls=%fused_computation.23 | convolution fusion | flops 1074790400 | bytes 9699328 | tf_op jit(solution)/shard_map/gts,tgd->sd/dot_general | solution.py:45
  79.9 7.5 %convolution_bitcast_fusion.1 = f32[256,4,128]{2,0,1:T(8,128)} fusion(bf16[4,256,4096]{1,2,0:T(8,128)(2,1)} %fusion.5, bf16[4096,256]{1,0:T(8,128)(2,1)S(1)} %bitcast.148), kind=kOutput, calls=%fused_computation.40 | convolution fusion | flops 1073741824 | bytes 9961472 | tf_op jit(solution)/shard_map/gts,sd->tgd/dot_general | solution.py:45
  87.5 4.3 %fusion.2 = bf16[4096,4,256]{2,0,1:T(8,128)(2,1)S(1)} fusion(f32[4096,256,4]{1,0,2:T(8,128)S(1)} %bitcast.137, f32[4,256]{1,0:T(4,128)S(1)} %log_add_fusion, pred[4096,256]{1,0:T(8,128)(4,1)S(1)} %bitcast.138), kind=kLoop, calls=%fused_computation.3 | loop fusion | flops 20971520 | bytes 26218496 | tf_op jit(solution)/shard_map/convert_element_type | solution.py:57
  91.8 2.8 %fusion.70 = bf16[8,2,256,128,1]{2,3,1,0,4:T(8,128)(2,1)S(1)} fusion(bf16[8,2,256,4,256]{4,2,1,0,3:T(8,128)(2,1)S(1)} %bitcast.143, bf16[256,4,128,1,1]{0,2,4,3,1:T(8,128)(2,1)S(1)} %bitcast.155), kind=kOutput, calls=%fused_computation.128 | convolution fusion | flops 1073741824 | bytes 9699328 | tf_op jit(solution)/shard_map/gts,tgd->sd/dot_general | solution.py:45
  94.8 2.3 copy.59
  97.1 2.1 fusion.25
  99.7 1.5 subtract_convert_fusion
  101.1 0.9 pad_maximum_fusion.2
  102.0 1.1 copy.57
  103.1 3.2 %fusion.11 = bf16[4096,512]{0,1:T(8,128)(2,1)} fusion(bf16[256,512]{0,1:T(8,128)(2,1)S(1)} %bitcast.149, bf16[256,4096]{1,0:T(8,128)(2,1)S(1)} %copy-done), kind=kOutput, calls=%fused_computation.16 | convolution fusion | flops 1075838976 | bytes 6553600 | tf_op jit(solution)/shard_map/dot_general | solution.py:148
  106.3 8.1 %reshape.322 = bf16[8,2,256,512]{2,1,0,3:T(2,128)(2,1)} reshape(bf16[4096,512]{0,1:T(8,128)(2,1)} %fusion.11) | data formatting | bytes 8388608 | tf_op jit(solution)/shard_map/reshape | solution.py:104
  114.4 11.4 %constant_dynamic-slice_fusion.3 = (bf16[8,1,256,512]{2,1,0,3:T(2,128)(2,1)}, bf16[8,1,256,512]{2,1,0,3:T(2,128)(2,1)}) fusion(bf16[8,2,256,512]{2,1,0,3:T(2,128)(2,1)} %reshape.322, s32[]{:T(128)S(6)} %select_n.93, s32[]{:T(128)S(6)} %select_n.94), kind=kLoop, calls=%fused_computation.109 | loop fusion | bytes 8388616 | tf_op jit(solution)/shard_map/jit(dynamic_index_in_dim)/dynamic_slice | solution.py:106
  125.8 10.5 %copy.79 = bf16[8,1,256,512]{3,2,0,1:T(8,128)(2,1)} copy(bf16[8,1,256,512]{2,1,0,3:T(2,128)(2,1)} %get-tuple-element.5) | data formatting | bytes 4194304
  136.3 2.6 %fusion.17 = bf16[8,256,256]{1,2,0:T(8,128)(2,1)} fusion(bf16[8,256,256]{1,2,0:T(8,128)(2,1)} %collective-permute-done.1, s32[]{:T(128)S(6)} %select_n.93, bf16[8,2,256,128]{2,3,0,1:T(8,128)(2,1)} %copy.59, bf16[8,2,256,128]{2,3,0,1:T(8,128)(2,1)S(1)} %bitcast.140), kind=kLoop, calls=%fused_computation.36 | loop fusion | flops 4194304 | bytes 4194308 | tf_op jit(solution)/shard_map/convert_element_type | solution.py:109
  138.9 4.1 %all-to-all-start.1 = ((bf16[8,256,256]{1,2,0:T(8,128)(2,1)}), bf16[8,256,256]{1,2,0:T(8,128)(2,1)S(1)}, u32[]{:S(2)}, u32[]{:S(2)}) async-start(bf16[8,256,256]{1,2,0:T(8,128)(2,1)} %fusion.17), calls=%async_computation.1 | async-start | bytes 2097152 | tf_op jit(solution)/shard_map/all_to_all | solution.py:113
  143.1 10.5 %copy.78 = bf16[8,1,256,512]{3,2,0,1:T(8,128)(2,1)} copy(bf16[8,1,256,512]{2,1,0,3:T(2,128)(2,1)} %get-tuple-element.4) | data formatting | bytes 4194304
  153.6 5.3 %all-to-all-done.1 = bf16[8,256,256]{1,2,0:T(8,128)(2,1)S(1)} async-done(((bf16[8,256,256]{1,2,0:T(8,128)(2,1)}), bf16[8,256,256]{1,2,0:T(8,128)(2,1)S(1)}, u32[]{:S(2)}, u32[]{:S(2)}) %all-to-all-start.1) | async-done | bytes 1048608 | tf_op jit(solution)/shard_map/all_to_all | solution.py:113
  160.0 3.9 %fusion.65 = f32[256,4096]{1,0:T(8,128)} fusion(bf16[4096,128]{1,0:T(8,128)(2,1)} %param.9, bf16[256,1,64]{0,2,1:T(8,128)(2,1)S(1)} %get-tuple-element.19, bf16[256,1,64]{0,2,1:T(8,128)(2,1)S(1)} %get-tuple-element.18), kind=kOutput, calls=%fused_computation.123 | convolution fusion | flops 268566528 | bytes 5308416 | tf_op jit(solution)/shard_map/dot_general | solution.py:173
  164.0 3.5 %fusion.15 = bf16[8,256,512]{2,1,0:T(8,128)(2,1)} fusion(bf16[8,256,512]{2,1,0:T(8,128)(2,1)} %collective-permute-done.2, bf16[8,1,256,512]{3,2,0,1:T(8,128)(2,1)S(1)} %copy-done.2), kind=kLoop, calls=%fused_computation.25 | loop fusion | flops 4194304 | bytes 6291456 | tf_op jit(solution)/shard_map/convert_element_type | solution.py:109
  167.5 4.9 %convolution_add_fusion = f32[256,4096]{1,0:T(8,128)S(1)} fusion(f32[256,4096]{1,0:T(8,128)} %fusion.65, bf16[256,512]{0,1:T(8,128)(2,1)S(1)} %bitcast.150, bf16[4096,512]{1,0:T(8,128)(2,1)} %param.8), kind=kOutput, calls=%fused_computation.17 | convolution fusion | flops 1074790400 | bytes 12845056 | tf_op jit(solution)/shard_map/dot_general | solution.py:159
  173.2 1.5 copy.91
  174.7 5.3 %all-to-all-start.2 = ((bf16[8,256,512]{2,1,0:T(8,128)(2,1)}), bf16[8,256,512]{2,1,0:T(8,128)(2,1)}, u32[]{:S(2)}, u32[]{:S(2)}) async-start(bf16[8,256,512]{2,1,0:T(8,128)(2,1)} %bitcast.144), calls=%async_computation.2 | async-start | bytes 4194304 | tf_op jit(solution)/shard_map/all_to_all | solution.py:113
  179.9 2.1 fusion.13
  182.1 4.6 %reshape.324 = bf16[8,2,256,256]{2,1,0,3:T(2,128)(2,1)} reshape(bf16[4096,256]{0,1:T(8,128)(2,1)} %fusion.13) | data formatting | bytes 4194304 | tf_op jit(solution)/shard_map/reshape | solution.py:104
  186.7 8.6 %constant_dynamic-slice_fusion.1 = (bf16[8,1,256,256]{2,1,0,3:T(2,128)(2,1)}, bf16[8,1,256,256]{2,1,0,3:T(2,128)(2,1)}) fusion(bf16[8,2,256,256]{2,1,0,3:T(2,128)(2,1)} %reshape.324, s32[]{:T(128)S(6)} %select_n.93, s32[]{:T(128)S(6)} %select_n.94), kind=kLoop, calls=%fused_computation.107 | loop fusion | bytes 4194312 | tf_op jit(solution)/shard_map/jit(dynamic_index_in_dim)/dynamic_slice | solution.py:106
  195.2 5.8 %copy.81 = bf16[8,1,256,256]{3,2,0,1:T(8,128)(2,1)} copy(bf16[8,1,256,256]{2,1,0,3:T(2,128)(2,1)} %get-tuple-element.7) | data formatting | bytes 2097152
  201.0 4.5 %copy.80 = bf16[8,1,256,256]{3,2,0,1:T(8,128)(2,1)S(1)} copy(bf16[8,1,256,256]{2,1,0,3:T(2,128)(2,1)} %get-tuple-element.6) | data formatting | bytes 2097152
  205.6 2.5 fusion.16
  208.0 1.6 all-to-all-done.2
  209.6 6.0 %all-to-all-start.3 = ((bf16[8,256,256]{2,1,0:T(8,128)(2,1)}), bf16[8,256,256]{2,1,0:T(8,128)(2,1)S(1)}, u32[]{:S(2)}, u32[]{:S(2)}) async-start(bf16[8,256,256]{2,1,0:T(8,128)(2,1)} %fusion.16), calls=%async_computation.4 | async-start | bytes 2097152 | tf_op jit(solution)/shard_map/all_to_all | solution.py:113
  215.6 2.7 %reduce_sum.51 = bf16[256,512]{1,0:T(8,128)(2,1)} reduce(bf16[8,256,512]{2,1,0:T(8,128)(2,1)} %all-to-all-done.2, bf16[]{:T(256)} %constant.106.clone.1), dimensions={0}, to_apply=%region_4.5 | reduce | flops 917504 | bytes 2359298 | tf_op jit(solution)/shard_map/reduce_sum | solution.py:114
  218.3 12.9 %all-to-all-done.3 = bf16[8,256,256]{2,1,0:T(8,128)(2,1)S(1)} async-done(((bf16[8,256,256]{2,1,0:T(8,128)(2,1)}), bf16[8,256,256]{2,1,0:T(8,128)(2,1)S(1)}, u32[]{:S(2)}, u32[]{:S(2)}) %all-to-all-start.3) | async-done | bytes 1048608 | tf_op jit(solution)/shard_map/all_to_all | solution.py:113
  232.1 13.2 %reduce-scatter.2.cloned.1.call-done = bf16[256,512]{1,0:T(8,128)(2,1)} async-done(((bf16[2048,512]{1,0:T(8,128)(2,1)}), bf16[256,512]{1,0:T(8,128)(2,1)}) %reduce-scatter.2.cloned.1.call-update) | async-done | bytes 262160 | tf_op jit(solution)/shard_map/reduce_scatter | solution.py:152
  245.3 1.8 convert_element_type.119
  (75 shorter events, 8.2 us)
Async XLA Ops:
  7.2 1.6 copy-start
  14.4 23.8 %all-to-all-start = ((bf16[8,256,256]{2,1,0:T(8,128)(2,1)}), bf16[8,256,256]{2,1,0:T(8,128)(2,1)}, u32[]{:S(2)}, u32[]{:S(2)}) async-start(bf16[8,256,256]{2,1,0:T(8,128)(2,1)} %broadcast_in_dim.76), calls=%async_computation | async-start | bytes 2097152 | tf_op jit(solution)/shard_map/all_to_all | solution.py:93
  22.3 16.5 %copy-start.14 = (s32[2,32]{1,0:T(2,128)S(1)}, s32[2,32]{1,0:T(2,128)}, u32[]{:S(2)}) copy-start(s32[2,32]{1,0:T(2,128)} %param.12) | copy-start | bytes 772
  22.3 16.9 %copy-start.11 = (bf16[256,512]{1,0:T(8,128)(2,1)S(1)}, bf16[256,512]{1,0:T(8,128)(2,1)}, u32[]{:S(2)}) copy-start(bf16[256,512]{1,0:T(8,128)(2,1)} %param.13) | copy-start | bytes 786436
  38.2 5.1 %collective-permute-start = (bf16[8,256,256]{2,1,0:T(8,128)(2,1)}, bf16[8,256,256]{2,1,0:T(8,128)(2,1)}, u32[]{:S(2)}, u32[]{:S(2)}) collective-permute-start(bf16[8,256,256]{2,1,0:T(8,128)(2,1)} %all-to-all-done), channel_id=1, source_target_pairs={{0,8},{8,0},{1,9},{9,1},{2,10},{10,2},{3,11},{11,3},{4,12},{12,4},... | collective-permute-start | bytes 3145736 | tf_op jit(solution)/shard_map/ppermute | solution.py:94
  42.7 0.7 copy-start.6
  43.3 2.1 copy-start.9
  43.3 2.1 copy-start.10
  48.4 5.7 %copy-start.1 = (f32[4096,256,4]{1,0,2:T(8,128)}, f32[4096,256,4]{1,0,2:T(8,128)S(1)}, u32[]{:S(2)}) copy-start(f32[4096,256,4]{1,0,2:T(8,128)S(1)} %get-tuple-element.26) | copy-start | bytes 50331652
  48.4 5.7 %copy-start.12 = (bf16[256,512]{0,1:T(8,128)(2,1)S(1)}, bf16[256,512]{0,1:T(8,128)(2,1)}, u32[]{:S(2)}) copy-start(bf16[256,512]{0,1:T(8,128)(2,1)} %copy.50) | copy-start | bytes 786436
  58.6 28.9 %slice-start = ((s8[16777216]{0:T(1024)(128)(4,1)}), s8[4194304]{0:T(1024)(128)(4,1)S(1)}, s32[]{:S(2)}) async-start(s8[16777216]{0:T(1024)(128)(4,1)} %bitcast.136), calls=%async_computation.6 | async-start | bytes 8388608
  58.6 28.9 %slice-start.1 = ((s8[16777216]{0:T(1024)(128)(4,1)}), s8[4194304]{0:T(1024)(128)(4,1)S(1)}, s32[]{:S(2)}) async-start(s8[16777216]{0:T(1024)(128)(4,1)} %bitcast.136), calls=%async_computation.7 | async-start | bytes 8388608
  58.6 28.9 %slice-start.2 = ((s8[16777216]{0:T(1024)(128)(4,1)}), s8[4194304]{0:T(1024)(128)(4,1)S(1)}, s32[]{:S(2)}) async-start(s8[16777216]{0:T(1024)(128)(4,1)} %bitcast.136), calls=%async_computation.8 | async-start | bytes 8388608
  72.8 14.7 %slice-start.3 = ((s8[16777216]{0:T(1024)(128)(4,1)}), s8[4194304]{0:T(1024)(128)(4,1)S(1)}, s32[]{:S(2)}) async-start(s8[16777216]{0:T(1024)(128)(4,1)} %bitcast.136), calls=%async_computation.9 | async-start | bytes 8388608
  87.5 4.4 %copy-start.13 = (bf16[256,512]{0,1:T(8,128)(2,1)S(1)}, bf16[256,512]{0,1:T(8,128)(2,1)}, u32[]{:S(2)}) copy-start(bf16[256,512]{0,1:T(8,128)(2,1)} %copy.50) | copy-start | bytes 786436
  94.7 5.0 %copy-start.7 = (f32[256,64]{1,0:T(8,128)S(1)}, f32[256,64]{1,0:T(8,128)}, u32[]{:S(2)}) copy-start(f32[256,64]{1,0:T(8,128)} %copy-done.6) | copy-start | bytes 196612
  94.7 5.0 %copy-start.8 = (f32[256,64]{1,0:T(8,128)S(1)}, f32[256,64]{1,0:T(8,128)}, u32[]{:S(2)}) copy-start(f32[256,64]{1,0:T(8,128)} %get-tuple-element.22) | copy-start | bytes 196612
  99.2 37.1 %collective-permute-start.1 = (bf16[8,256,256]{1,2,0:T(8,128)(2,1)}, bf16[8,256,256]{1,2,0:T(8,128)(2,1)}, u32[]{:S(2)}, u32[]{:S(2)}) collective-permute-start(bf16[8,256,256]{1,2,0:T(8,128)(2,1)} %fusion.25), channel_id=1, source_target_pairs={{0,8},{8,0},{1,9},{9,1},{2,10},{10,2},{3,11},{11,3},{4,12},{12,4},... | collective-permute-start | bytes 3145736 | tf_op jit(solution)/shard_map/ppermute | solution.py:108
  136.3 27.7 %collective-permute-start.2 = (bf16[8,256,512]{2,1,0:T(8,128)(2,1)}, bf16[8,256,512]{2,1,0:T(8,128)(2,1)}, u32[]{:S(2)}, u32[]{:S(2)}) collective-permute-start(bf16[8,256,512]{2,1,0:T(8,128)(2,1)} %bitcast.151), channel_id=1, source_target_pairs={{0,8},{8,0},{1,9},{9,1},{2,10},{10,2},{3,11},{11,3},{4,12},{12,4},... | collective-permute-start | bytes 6291464 | tf_op jit(solution)/shard_map/ppermute | solution.py:108
  138.9 19.9 %all-to-all-start.1 = ((bf16[8,256,256]{1,2,0:T(8,128)(2,1)}), bf16[8,256,256]{1,2,0:T(8,128)(2,1)S(1)}, u32[]{:S(2)}, u32[]{:S(2)}) async-start(bf16[8,256,256]{1,2,0:T(8,128)(2,1)} %fusion.17), calls=%async_computation.1 | async-start | bytes 2097152 | tf_op jit(solution)/shard_map/all_to_all | solution.py:113
  143.0 102.3 %reduce-scatter.2.cloned.1.call-start = ((), (), s32[]{:S(2)}) async-start(), calls=%async_computation.5 | async-start | bytes 2359296 | tf_op jit(solution)/shard_map/reduce_scatter | solution.py:152
  158.8 5.1 %copy-start.2 = (bf16[8,1,256,512]{3,2,0,1:T(8,128)(2,1)S(1)}, bf16[8,1,256,512]{3,2,0,1:T(8,128)(2,1)}, u32[]{:S(2)}) copy-start(bf16[8,1,256,512]{3,2,0,1:T(8,128)(2,1)} %copy.78) | copy-start | bytes 6291460
  159.0 0.7 copy-start.4
  167.5 4.9 %copy-start.5 = (f32[256,256]{0,1:T(8,128)S(1)}, f32[256,256]{0,1:T(8,128)}, u32[]{:S(2)}) copy-start(f32[256,256]{0,1:T(8,128)} %copy-done.4) | copy-start | bytes 786436
  167.5 4.9 %copy-start.3 = (bf16[4096,128]{1,0:T(8,128)(2,1)S(1)}, bf16[4096,128]{1,0:T(8,128)(2,1)}, u32[]{:S(2)}) copy-start(bf16[4096,128]{1,0:T(8,128)(2,1)} %param.10) | copy-start | bytes 3145732
  174.7 35.0 %all-to-all-start.2 = ((bf16[8,256,512]{2,1,0:T(8,128)(2,1)}), bf16[8,256,512]{2,1,0:T(8,128)(2,1)}, u32[]{:S(2)}, u32[]{:S(2)}) async-start(bf16[8,256,512]{2,1,0:T(8,128)(2,1)} %bitcast.144), calls=%async_computation.2 | async-start | bytes 4194304 | tf_op jit(solution)/shard_map/all_to_all | solution.py:113
  201.0 4.5 %collective-permute-start.3 = (bf16[8,256,256]{2,1,0:T(8,128)(2,1)}, bf16[8,256,256]{2,1,0:T(8,128)(2,1)}, u32[]{:S(2)}, u32[]{:S(2)}) collective-permute-start(bf16[8,256,256]{2,1,0:T(8,128)(2,1)} %bitcast.36), channel_id=1, source_target_pairs={{0,8},{8,0},{1,9},{9,1},{2,10},{10,2},{3,11},{11,3},{4,12},{12,4},... | collective-permute-start | bytes 3145736 | tf_op jit(solution)/shard_map/ppermute | solution.py:108
  209.6 21.6 %all-to-all-start.3 = ((bf16[8,256,256]{2,1,0:T(8,128)(2,1)}), bf16[8,256,256]{2,1,0:T(8,128)(2,1)S(1)}, u32[]{:S(2)}, u32[]{:S(2)}) async-start(bf16[8,256,256]{2,1,0:T(8,128)(2,1)} %fusion.16), calls=%async_computation.4 | async-start | bytes 2097152 | tf_op jit(solution)/shard_map/all_to_all | solution.py:113
Sparse Core Ops, SparseCore 0:
  167.6 77.6 reduce-scatter.1
